TPU v7x, 256 devices: a whole 4x4x8 slice. The times are simulated.
256 devices in a mesh: node: 16 (over y, x_hi, core), tm: 16 (over z, x_lo).
Axes of the slice: x: 4 (x_hi: 2, x_lo: 2; x = x_hi * 2 + x_lo), y: 4, z: 8, core: 2. Of those that a mesh axis runs over, the one named last changes fastest.
Arguments:
- observed: bfloat16 [65536, 16384], P('node', 'tm'), may hold values from 0.5 to 32
- node_factor: bfloat16 [64, 65536], P(None, ('node', 'tm')), may hold values from 0.19921875 to 1
- time_factor: bfloat16 [64, 1024], P(None, 'tm'), may hold values from 0.19921875 to 1
- species_factor: bfloat16 [64, 16], replicated, may hold values from 0.19921875 to 1
Outputs:
- grad_node: float32 [64, 65536], P(None, ('node', 'tm'))
- grad_time: float32 [64, 1024], P(None, 'tm')
- grad_species: float32 [64, 16], replicated
All inputs are finite; a program needn't handle non-finite values.
Results may differ from a plain program's by a relative error of at most 0.0017.
Values may be sent and summed in bfloat16 or wider, within the bound.
No kernel may reach another device: no remote copies, remote signals or barrier semaphores. Data moves between devices by JAX's collectives and lax.ppermute only.
A program may use at most 64 MiB of HBM per device.

v0:
```python
import math
import jax
import jax.numpy as jnp
from jax import lax
from jax.sharding import PartitionSpec as P


def widen(values):
    return lax.optimization_barrier(values).astype(jnp.float32)


def shards(observed, node_factor, time_factor, species_factor):
    factor_rank = node_factor.shape[0]
    time_vals = time_factor.astype(jnp.float32)
    species_vals = species_factor.astype(jnp.float32)
    time_dev = time_vals.shape[1]
    species = species_vals.shape[1]
    node_rows = observed.shape[0]
    flat_width = observed.shape[1]
    khatri = (
        (time_vals[:, :, None] * species_vals[:, None, :])
        .reshape(factor_rank, flat_width)
        .astype(jnp.bfloat16)
    )
    khatri_wide = widen(khatri)
    factor_wide = lax.all_gather(node_factor, "tm", axis=1, tiled=True).astype(jnp.float32)
    modelled = lax.dot_general(
        factor_wide, khatri_wide, (((0,), (0,)), ((), ())), precision=lax.Precision.HIGHEST
    )
    derivative = ((modelled - observed.astype(jnp.float32)) / (modelled * modelled)).astype(
        jnp.bfloat16
    )
    derivative_wide = widen(derivative)
    node_part = lax.dot_general(
        khatri_wide, derivative_wide, (((1,), (1,)), ((), ())), precision=lax.Precision.HIGHEST
    )
    node_grads = node_part
    contracted = lax.dot_general(
        derivative_wide, factor_wide, (((0,), (1,)), ((), ())), precision=lax.Precision.HIGHEST
    )
    node_grads, contracted = (node_grads, contracted)
    tm_count = lax.axis_size("tm")
    steps_all = time_dev * tm_count
    nodes_all = node_rows * lax.axis_size("node")
    share_rows = node_rows // tm_count
    summed = lax.psum(node_grads, "tm")
    grad_node = lax.dynamic_slice_in_dim(summed, lax.axis_index("tm") * share_rows, share_rows, 1)
    grad_node = grad_node / math.sqrt(steps_all * species)
    by_step = contracted.reshape(time_dev, species, factor_rank)
    time_grad = jnp.einsum("tsr,rs->rt", by_step, species_vals, precision=lax.Precision.HIGHEST)
    species_grad = jnp.einsum("tsr,rt->rs", by_step, time_vals, precision=lax.Precision.HIGHEST)
    time_grad = lax.psum(time_grad, "node")
    species_grad = lax.psum(species_grad, ("node", "tm"))
    grad_time = time_grad / math.sqrt(nodes_all * species)
    grad_species = species_grad / math.sqrt(nodes_all * steps_all)
    return (grad_node, grad_time, grad_species)


def solution(mesh):
    in_specs = (P("node", "tm"), P(None, ("node", "tm")), P(None, "tm"), P())
    out_specs = (P(None, ("node", "tm")), P(None, "tm"), P())
    return jax.shard_map(shards, mesh=mesh, in_specs=in_specs, out_specs=out_specs, check_vma=False)
```

profile of v0, /device:TPU:32, one launch (start us, length us, event | category | flops | bytes accessed | tf_op | source)
XLA Modules:
  0.0 226.5 jit_solution(11420919624136938555)
XLA Ops:
  7.2 0.0 all-reduce.2.cloned.1.call-start
  7.2 0.7 convert_element_type.22
  7.9 0.8 copy.9
  8.7 0.1 multiply_convert_fusion
  8.8 36.8 %all_gather.3 = bf16[64,4096]{1,0:T(8,128)(2,1)S(1)} all-gather(bf16[64,256]{1,0:T(8,128)(2,1)} %param.5), channel_id=1, replica_groups=mesh['node'=16,'tm'=16] {'tm'}, dimensions={1}, use_global_device_ids=true | all-gather | bytes 557056 | tf_op jit(solution)/shard_map/all_gather | solution.py:26
  45.5 11.3 %copy.10 = bf16[4096,1024]{0,1:T(8,128)(2,1)} copy(bf16[4096,1024]{1,0:T(8,128)(2,1)} %param.4) | data formatting | bytes 16777216 | tf_op args[0]
  56.8 5.7 %fusion.1 = bf16[4096,1024]{0,1:T(8,128)(2,1)S(1)} fusion(bf16[4096,1024]{0,1:T(8,128)(2,1)} %copy.10, bf16[64,1024]{0,1:T(8,128)(2,1)S(1)} %bitcast.23, bf16[64,4096]{1,0:T(8,128)(2,1)S(1)} %all_gather.3), kind=kOutput, calls=%fused_computation.3 | convolution fusion | flops 557842432 | bytes 17432576 | tf_op jit(solution)/shard_map/dot_general | solution.py:27
  62.5 0.0 copy-start
  62.5 3.2 %copy-done = bf16[4096,1024]{0,1:T(8,128)(2,1)} copy-done((bf16[4096,1024]{0,1:T(8,128)(2,1)}, bf16[4096,1024]{0,1:T(8,128)(2,1)S(1)}, u32[]{:S(2)}) %copy-start) | copy-done | bytes 8388632
  65.7 2.6 %fusion.2 = f32[64,4096]{1,0:T(8,128)} fusion(bf16[64,1024]{0,1:T(8,128)(2,1)S(1)} %bitcast.24, bf16[4096,1024]{0,1:T(8,128)(2,1)S(1)} %fusion.1), kind=kOutput, calls=%fused_computation.10 | convolution fusion | flops 536870912 | bytes 9568256 | tf_op jit(solution)/shard_map/dot_general | solution.py:34
  68.3 0.0 all-reduce.2.cloned.1.call-update
  68.3 5.7 %multiply_reduce_fusion.1 = (f32[64,64]{0,1:T(8,128)S(1)}, f32[1024,64]{1,0:T(8,128)S(1)}) fusion(f32[64,16]{0,1:T(8,128)S(1)} %convert_element_type.22, bf16[4096,1024]{0,1:T(8,128)(2,1)} %copy-done, bf16[64,4096]{1,0:T(8,128)(2,1)S(1)} %all_gather.3), kind=kOutput, calls=%fused_computation.5 | convolution fusion | flops 536997888 | bytes 9195520 | tf_op jit(solution)/shard_map/dot_general | solution.py:38
  74.0 0.1 copy.18
  74.1 0.1 multiply_reduce_fusion
  74.2 76.9 %psum.23 = f32[64,16]{0,1:T(8,128)S(1)} all-reduce(f32[64,16]{0,1:T(8,128)S(1)} %multiply_reduce_fusion), channel_id=1, replica_groups=mesh['node'=16,'tm'=16] {'node','tm'}, use_global_device_ids=true, to_apply=%region_2.0 | all-reduce | flops 1024 | bytes 8192 | tf_op jit(solution)/shard_map/psum | solution.py:53
  151.1 65.8 %psum.22 = f32[64,64]{1,0:T(8,128)S(1)} all-reduce(f32[64,64]{1,0:T(8,128)S(1)} %copy.18), channel_id=1, replica_groups=mesh['node'=16,'tm'=16] {'node'}, use_global_device_ids=true, to_apply=%region_1.0 | all-reduce | flops 4096 | bytes 32768 | tf_op jit(solution)/shard_map/psum | solution.py:52
  217.0 0.6 broadcast_multiply_fusion.1
  217.6 0.6 broadcast_multiply_fusion
  218.2 0.0 all-reduce.2.cloned.1.call-done
  218.2 1.5 dynamic-slice_multiply_fusion
Async XLA Ops:
  7.2 211.0 %all-reduce.2.cloned.1.call-start = ((), (), s32[]{:S(2)}) async-start(), calls=%async_computation | async-start | bytes 2097152 | tf_op jit(solution)/shard_map/psum | solution.py:46
  62.5 3.2 %copy-start = (bf16[4096,1024]{0,1:T(8,128)(2,1)}, bf16[4096,1024]{0,1:T(8,128)(2,1)S(1)}, u32[]{:S(2)}) copy-start(bf16[4096,1024]{0,1:T(8,128)(2,1)S(1)} %fusion.1) | copy-start | bytes 25165828
Sparse Core Ops, SparseCore 0:
  68.4 138.8 all-reduce.1
where the time goes:
time: 227 us; the launch traced here: 226 us
  blocking collectives  180 us (79%)
  local copies, waits for them, and re-layouts  15.3 us (7%)
  between operations  14.1 us (6%)
  matrix products  14 us (6%)
  other arithmetic  3.56 us (2%)
    psum x1, blocking collectives, shards(): species_grad = lax.psum(species_grad, ('node', 'tm'))  76.9 us
    psum x1, blocking collectives, shards(): time_grad = lax.psum(time_grad, 'node')  65.8 us
    all_gather x1, blocking collectives, shards(): lax.all_gather(node_factor, 'tm', axis=1, tiled=True).astype(jnp.float32)  36.8 us
    unnamed x3, local copies, waits for them, and re-layouts  14.5 us
    dot_general x1, matrix products, shards(): lax.dot_general(derivative_wide, factor_wide, (((0,), (1,)), ((), ())), p...  5.71 us
    dot_general x1, matrix products, shards(): lax.dot_general(factor_wide, khatri_wide, (((0,), (0,)), ((), ())), preci...  5.67 us
  transfers between devices with their start and end apart: 1, of which 0 were waited for; matrix products, arithmetic and copies ran while one was open for 3% of the time, Pallas kernels for 0%

commit v1 on v0

--- a/solution.py
+++ b/solution.py
@@ -23,7 +23,9 @@
         .astype(jnp.bfloat16)
     )
     khatri_wide = widen(khatri)
-    factor_wide = lax.all_gather(node_factor, "tm", axis=1, tiled=True).astype(jnp.float32)
+    factor_wide = jnp.concatenate(
+        lax.all_to_all(jnp.stack([node_factor] * lax.axis_size("tm")), "tm", 0, 0), axis=1
+    ).astype(jnp.float32)
     modelled = lax.dot_general(
         factor_wide, khatri_wide, (((0,), (0,)), ((), ())), precision=lax.Precision.HIGHEST
     )

time: 227 us -> 205 us (0.903)
  blocking collectives: 180 us -> 143 us
  starting transfers between devices: 0.04 us -> 9.55 us
  local copies, waits for them, and re-layouts: 15.3 us -> 17.6 us
    all_gather x1 -> x0, blocking collectives: 36.8 us -> none  [shards(): lax.all_gather(node_factor, 'tm', axis=1, tiled=True).astype(jnp.float32)]
    all_to_all x0 -> x1, starting transfers between devices: none -> 9.51 us  [shards(): lax.all_to_all(jnp.stack([node_factor] * lax.axis_size('tm')), 'tm', 0, 0)]
  transfers between devices with their start and end apart: 1 -> 2, of which waited for: 0 -> 1; matrix products, arithmetic and copies ran while one was open for 3% -> 10% of each run, Pallas kernels for 0% -> 0%
where the time goes in v1:
time: 205 us; the launch traced here: 204 us
  blocking collectives  143 us (70%)
  local copies, waits for them, and re-layouts  17.6 us (9%)
  between operations  14.1 us (7%)
  matrix products  14 us (7%)
  starting transfers between devices  9.55 us (5%)
  other arithmetic  3.57 us (2%)
  waiting for transfers between devices  2.15 us (1%)
    psum x1, blocking collectives, shards(): species_grad = lax.psum(species_grad, ('node', 'tm'))  77.3 us
    psum x1, blocking collectives, shards(): time_grad = lax.psum(time_grad, 'node')  65.5 us
    unnamed x3, local copies, waits for them, and re-layouts  14.5 us
    all_to_all x1, starting transfers between devices, shards(): lax.all_to_all(jnp.stack([node_factor] * lax.axis_size('tm')), 'tm', 0, 0)  9.51 us
    dot_general x1, matrix products, shards(): lax.dot_general(derivative_wide, factor_wide, (((0,), (1,)), ((), ())), p...  5.71 us
    dot_general x1, matrix products, shards(): lax.dot_general(factor_wide, khatri_wide, (((0,), (0,)), ((), ())), preci...  5.68 us
  transfers between devices with their start and end apart: 2, of which 1 were waited for; matrix products, arithmetic and copies ran while one was open for 10% of the time, Pallas kernels for 0%

profile of v1, /device:TPU:32, one launch (start us, length us, event | category | flops | bytes accessed | tf_op | source)
XLA Modules:
  0.0 203.7 jit_solution(12009276911227099525)
XLA Ops:
  7.2 1.7 stack.2
  8.8 9.5 %all-to-all-start = ((bf16[16,64,256]{2,1,0:T(8,128)(2,1)}), bf16[16,64,256]{2,1,0:T(8,128)(2,1)S(1)}, u32[]{:S(2)}, u32[]{:S(2)}) async-start(bf16[16,64,256]{2,1,0:T(8,128)(2,1)} %stack.2), calls=%async_computation | async-start | bytes 1048576 | tf_op jit(solution)/shard_map/all_to_all | solution.py:27
  18.3 0.0 all-reduce.2.cloned.1.call-start
  18.4 0.7 convert_element_type.22
  19.1 0.8 copy.11
  19.9 0.1 multiply_convert_fusion
  19.9 11.3 %copy.13 = bf16[4096,1024]{0,1:T(8,128)(2,1)} copy(bf16[4096,1024]{1,0:T(8,128)(2,1)} %param.4) | data formatting | bytes 16777216 | tf_op args[0]
  31.2 2.1 %all-to-all-done = bf16[16,64,256]{2,1,0:T(8,128)(2,1)S(1)} async-done(((bf16[16,64,256]{2,1,0:T(8,128)(2,1)}), bf16[16,64,256]{2,1,0:T(8,128)(2,1)S(1)}, u32[]{:S(2)}, u32[]{:S(2)}) %all-to-all-start) | async-done | bytes 524320 | tf_op jit(solution)/shard_map/all_to_all | solution.py:27
  33.3 0.3 copy.12
  33.6 0.2 reshape.25
  33.9 5.7 %fusion.1 = bf16[4096,1024]{0,1:T(8,128)(2,1)S(1)} fusion(bf16[4096,1024]{0,1:T(8,128)(2,1)} %copy.13, bf16[64,1024]{0,1:T(8,128)(2,1)S(1)} %bitcast.29, bf16[64,4096]{1,0:T(8,128)(2,1)S(1)} %bitcast.31), kind=kOutput, calls=%fused_computation.3 | convolution fusion | flops 557842432 | bytes 17432576 | tf_op jit(solution)/shard_map/dot_general | solution.py:29
  39.6 0.0 copy-start
  39.6 3.2 %copy-done = bf16[4096,1024]{0,1:T(8,128)(2,1)} copy-done((bf16[4096,1024]{0,1:T(8,128)(2,1)}, bf16[4096,1024]{0,1:T(8,128)(2,1)S(1)}, u32[]{:S(2)}) %copy-start) | copy-done | bytes 8388632
  42.8 2.6 %fusion.2 = f32[64,4096]{1,0:T(8,128)} fusion(bf16[64,1024]{0,1:T(8,128)(2,1)S(1)} %bitcast.30, bf16[4096,1024]{0,1:T(8,128)(2,1)S(1)} %fusion.1), kind=kOutput, calls=%fused_computation.10 | convolution fusion | flops 536870912 | bytes 9568256 | tf_op jit(solution)/shard_map/dot_general | solution.py:36
  45.4 0.0 all-reduce.2.cloned.1.call-update
  45.4 5.7 %multiply_reduce_fusion.1 = (f32[64,64]{0,1:T(8,128)S(1)}, f32[64,16,64]{2,1,0:T(8,128)S(1)}) fusion(f32[64,16]{0,1:T(8,128)S(1)} %convert_element_type.22, bf16[64,16,4096]{2,1,0:T(8,128)(2,1)} %bitcast.26, bf16[64,4096,1]{1,0,2:T(8,128)(2,1)S(1)} %reshape.25), kind=kOutput, calls=%fused_computation.5 | convolution fusion | flops 536997888 | bytes 9195520 | tf_op jit(solution)/shard_map/dot_general | solution.py:40
  51.2 0.1 copy.19
  51.2 0.1 multiply_reduce_fusion
  51.4 77.3 %psum.23 = f32[64,16]{0,1:T(8,128)S(1)} all-reduce(f32[64,16]{0,1:T(8,128)S(1)} %multiply_reduce_fusion), channel_id=1, replica_groups=mesh['node'=16,'tm'=16] {'node','tm'}, use_global_device_ids=true, to_apply=%region_2.0 | all-reduce | flops 1024 | bytes 8192 | tf_op jit(solution)/shard_map/psum | solution.py:55
  128.7 65.5 %psum.22 = f32[64,64]{1,0:T(8,128)S(1)} all-reduce(f32[64,64]{1,0:T(8,128)S(1)} %copy.19), channel_id=1, replica_groups=mesh['node'=16,'tm'=16] {'node'}, use_global_device_ids=true, to_apply=%region_1.0 | all-reduce | flops 4096 | bytes 32768 | tf_op jit(solution)/shard_map/psum | solution.py:54
  194.1 0.6 broadcast_multiply_fusion.1
  194.7 0.6 broadcast_multiply_fusion
  195.3 0.0 all-reduce.2.cloned.1.call-done
  195.3 1.5 dynamic-slice_multiply_fusion
  (1 shorter events, 0.0 us)
Async XLA Ops:
  8.8 24.5 %all-to-all-start = ((bf16[16,64,256]{2,1,0:T(8,128)(2,1)}), bf16[16,64,256]{2,1,0:T(8,128)(2,1)S(1)}, u32[]{:S(2)}, u32[]{:S(2)}) async-start(bf16[16,64,256]{2,1,0:T(8,128)(2,1)} %stack.2), calls=%async_computation | async-start | bytes 1048576 | tf_op jit(solution)/shard_map/all_to_all | solution.py:27
  18.3 177.0 %all-reduce.2.cloned.1.call-start = ((), (), s32[]{:S(2)}) async-start(), calls=%async_computation.1 | async-start | bytes 2097152 | tf_op jit(solution)/shard_map/psum | solution.py:48
  39.6 3.2 %copy-start = (bf16[4096,1024]{0,1:T(8,128)(2,1)}, bf16[4096,1024]{0,1:T(8,128)(2,1)S(1)}, u32[]{:S(2)}) copy-start(bf16[4096,1024]{0,1:T(8,128)(2,1)S(1)} %fusion.1) | copy-start | bytes 25165828
Sparse Core Ops, SparseCore 0:
  45.6 138.0 all-reduce.1

commit v2 on v0

--- a/solution.py
+++ b/solution.py
@@ -50,7 +50,7 @@
     time_grad = jnp.einsum("tsr,rs->rt", by_step, species_vals, precision=lax.Precision.HIGHEST)
     species_grad = jnp.einsum("tsr,rt->rs", by_step, time_vals, precision=lax.Precision.HIGHEST)
     time_grad = lax.psum(time_grad, "node")
-    species_grad = lax.psum(species_grad, ("node", "tm"))
+    species_grad = jnp.sum(lax.all_gather(species_grad, ("node", "tm")), axis=0)
     grad_time = time_grad / math.sqrt(nodes_all * species)
     grad_species = species_grad / math.sqrt(nodes_all * steps_all)
     return (grad_node, grad_time, grad_species)

time: 227 us -> 809 us (3.56)
  waiting for transfers between devices: 0.02 us -> 652 us
  blocking collectives: 180 us -> 102 us
    all_gather x0 -> x1, waiting for transfers between devices: none -> 586 us  [shards(): species_grad = jnp.sum(lax.all_gather(species_grad, ('node', 'tm')), axis=0)]
    psum x1 -> x0, blocking collectives: 76.9 us -> none  [shards(): species_grad = lax.psum(species_grad, ('node', 'tm'))]
    psum x1, waiting for transfers between devices: 0.01 us -> 66.5 us  [shards(): summed = lax.psum(node_grads, 'tm')]
  transfers between devices with their start and end apart: 1 -> 2, of which waited for: 0 -> 2; matrix products, arithmetic and copies ran while one was open for 3% -> 1% of each run, Pallas kernels for 0% -> 0%
where the time goes in v2:
time: 809 us; the launch traced here: 805 us
  waiting for transfers between devices  652 us (81%)
  blocking collectives  102 us (13%)
  between operations  15.5 us (2%)
  local copies, waits for them, and re-layouts  15.3 us (2%)
  matrix products  13.9 us (2%)
    all_gather x1, waiting for transfers between devices, shards(): species_grad = jnp.sum(lax.all_gather(species_grad, ('node', 'tm')), axis=0)  586 us
    psum x1, waiting for transfers between devices, shards(): summed = lax.psum(node_grads, 'tm')  66.5 us
    psum x1, blocking collectives, shards(): time_grad = lax.psum(time_grad, 'node')  65.5 us
    all_gather x1, blocking collectives, shards(): lax.all_gather(node_factor, 'tm', axis=1, tiled=True).astype(jnp.float32)  36.8 us
  transfers between devices with their start and end apart: 2, of which 2 were waited for; matrix products, arithmetic and copies ran while one was open for 1% of the time, Pallas kernels for 0%

profile of v2, /device:TPU:32, one launch (start us, length us, event | category | flops | bytes accessed | tf_op | source)
XLA Modules:
  0.0 805.3 jit_solution(5320316701728149048)
XLA Ops:
  8.0 0.0 all-reduce.2.cloned.1.call-start
  8.0 0.7 convert_element_type.22
  8.7 0.8 copy.12
  9.5 0.1 multiply_convert_fusion
  9.6 36.8 %all_gather.9 = bf16[64,4096]{1,0:T(8,128)(2,1)S(1)} all-gather(bf16[64,256]{1,0:T(8,128)(2,1)} %param.5), channel_id=1, replica_groups=mesh['node'=16,'tm'=16] {'tm'}, dimensions={1}, use_global_device_ids=true | all-gather | bytes 557056 | tf_op jit(solution)/shard_map/all_gather | solution.py:26
  46.4 11.3 %copy.13 = bf16[4096,1024]{0,1:T(8,128)(2,1)} copy(bf16[4096,1024]{1,0:T(8,128)(2,1)} %param.4) | data formatting | bytes 16777216 | tf_op args[0]
  57.6 5.6 fusion.1
  63.3 0.0 copy-start
  63.3 3.2 copy-done
  66.5 2.6 fusion.2
  69.1 0.0 all-reduce.2.cloned.1.call-update
  69.1 0.0 all-gather.4.cloned.1.call-start
  69.1 5.7 multiply_reduce_fusion.1
  74.8 0.7 multiply_reduce_fusion
  75.6 0.0 all-gather.4.cloned.1.call-update
  75.6 0.1 copy.21
  75.7 65.5 %psum.15 = f32[64,64]{1,0:T(8,128)S(1)} all-reduce(f32[64,64]{1,0:T(8,128)S(1)} %copy.21), channel_id=1, replica_groups=mesh['node'=16,'tm'=16] {'node'}, use_global_device_ids=true, to_apply=%region_1.0 | all-reduce | flops 4096 | bytes 32768 | tf_op jit(solution)/shard_map/psum | solution.py:52
  141.2 0.6 broadcast_multiply_fusion
  141.8 66.5 %all-reduce.2.cloned.1.call-done = f32[64,4096]{1,0:T(8,128)} async-done(((f32[64,4096]{1,0:T(8,128)}), f32[64,4096]{1,0:T(8,128)}) %all-reduce.2.cloned.1.call-update) | async-done | bytes 1048592 | tf_op jit(solution)/shard_map/psum | solution.py:46
  208.2 1.5 dynamic-slice_multiply_fusion
  209.7 585.6 %all-gather.4.cloned.1.call-done = f32[256,64,16]{1,2,0:T(8,128)} async-done(((f32[1,64,16]{1,2,0:T(8,128)}), f32[256,64,16]{1,2,0:T(8,128)}) %all-gather.4.cloned.1.call-update) | async-done | bytes 1048592 | tf_op jit(solution)/shard_map/all_gather | solution.py:53
  795.3 1.9 reduce_sum.9
  797.2 0.6 broadcast_multiply_fusion.1
Async XLA Ops:
  8.0 200.3 %all-reduce.2.cloned.1.call-start = ((), (), s32[]{:S(2)}) async-start(), calls=%async_computation | async-start | bytes 2097152 | tf_op jit(solution)/shard_map/psum | solution.py:46
  63.3 3.2 copy-start
  69.1 726.3 %all-gather.4.cloned.1.call-start = ((), (), s32[]{:S(2)}) async-start(), calls=%async_computation.1 | async-start | bytes 2105344 | tf_op jit(solution)/shard_map/all_gather | solution.py:53
Sparse Core Ops, SparseCore 0:
  69.2 138.9 all-reduce.1
Sparse Core Ops, SparseCore 1:
  75.7 719.6 all-gather.3
